TPU v7x, 256 devices: a whole 4x4x8 slice. The times are simulated.
256 devices in a mesh: grp: 8 (over y_hi, x), dom: 32 (over y_lo, z, core).
Axes of the slice: x: 4, y: 4 (y_hi: 2, y_lo: 2; y = y_hi * 2 + y_lo), z: 8, core: 2. Of those that a mesh axis runs over, the one named last changes fastest.
Arguments:
- fine_matrix_blocks: bfloat16 [16384, 64, 768], P(('grp', 'dom')), may hold values from -0.21875 to 0.21875
- prolongator: bfloat16 [16384, 64, 64], P(('grp', 'dom')), may hold values from -1.5 to 1.5
- block_columns: int32 [16384, 12], P(('grp', 'dom')), may hold values from 0 to 16383, as said below
- block_aggregates: int32 [16384, 12], P(('grp', 'dom')), may hold values from 0 to 1023, as said below
- live_counts: int32 [256], P(('grp', 'dom')), may hold values from 16 to 64, as said below
Outputs:
- coarse_operator: float32 [1024, 64, 768], P('dom')
Inputs may be any that keep to these rules, and one draw needn't show every extreme that they name: live_counts[p] counts the first slots of partition p that hold block rows; some partition has 64 and some has 16. `block_columns`: entry 0 of row i is i itself. For a live row of partition p, every entry is a live row of partition p - 1, p or p + 1 (only partitions that exist); entries may repeat, and repeated blocks add. block_aggregates[i, k] is the aggregate of row block_columns[i, k]. Every row of partition p, with g = p // 32 and q = p % 32, has an aggregate from (((q + 4 * g) % 32) * 8 + g) * 4 to that number plus 4 - 1.
All inputs are finite; a program needn't handle non-finite values.
Results may differ from a plain program's by a relative error of at most 0.0029.
Values may be sent and summed in bfloat16 or wider, within the bound.
No kernel may reach another device: no remote copies, remote signals or barrier semaphores. Data moves between devices by JAX's collectives and lax.ppermute only.
A program may use at most 192 MiB of HBM per device.

v0:
```python
import jax
import jax.numpy as jnp
from jax import lax
from jax.sharding import PartitionSpec as P

AGG_DEV = 4


def extended(block, sides, width):
    for axis, dim in sides:
        count = lax.axis_size(axis)
        forward = [(i, i + 1) for i in range(count - 1)]
        backward = [(target, source) for source, target in forward]
        low = lax.ppermute(
            lax.slice_in_dim(block, block.shape[dim] - width, None, axis=dim), axis, forward
        )
        high = lax.ppermute(lax.slice_in_dim(block, 0, width, axis=dim), axis, backward)
        block = jnp.concatenate([low, block, high], axis=dim)
    return block


def local(fine_matrix_blocks, prolongator, block_columns, block_aggregates, live_counts):
    capacity = fine_matrix_blocks.shape[0]
    block_width = prolongator.shape[1]
    row_blocks = block_columns.shape[1]
    slot_width = 3 * AGG_DEV
    position = lax.axis_index(("grp", "dom"))
    ghosts = extended(prolongator, ((("grp", "dom"), 0),), capacity)
    local_rows = block_columns - (position - 1) * capacity
    gathered = jnp.take(ghosts, local_rows, axis=0)
    matrix_view = fine_matrix_blocks.reshape(capacity, block_width, row_blocks, block_width)
    products = jnp.einsum(
        "ixky,ikyz->ixkz", matrix_view, gathered, preferred_element_type=jnp.float32
    )
    coarse_slot = AGG_DEV * (local_rows // capacity) + block_aggregates % AGG_DEV
    live_rows = jnp.arange(capacity) < live_counts[0]
    slot_select = (coarse_slot[:, :, None] == jnp.arange(slot_width)[None, None, :]) & live_rows[
        :, None, None
    ]
    row_sums = jnp.einsum(
        "ikt,ixkz->ixtz", slot_select.astype(jnp.float32), products, precision=lax.Precision.HIGHEST
    )
    row_sums = row_sums.astype(jnp.bfloat16).reshape(
        capacity * block_width, slot_width * block_width
    )
    row_select = (block_aggregates[:, 0:1] % AGG_DEV == jnp.arange(AGG_DEV)[None, :]) & live_rows[
        :, None
    ]
    spread = row_select.astype(jnp.bfloat16)[:, None, :, None] * prolongator[:, :, None, :]
    spread = spread.reshape(capacity * block_width, AGG_DEV * block_width)
    coarse = lax.dot_general(
        spread, row_sums, (((0,), (0,)), ((), ())), preferred_element_type=jnp.float32
    )
    groups_count = lax.axis_size("grp")
    places = lax.axis_size("dom")
    step_stride = places // groups_count
    pairs = [
        (g * places + q, g * places + (q + step_stride * g) % places)
        for g in range(groups_count)
        for q in range(places)
    ]
    rotated = lax.ppermute(coarse.astype(jnp.bfloat16), ("grp", "dom"), pairs)
    result = lax.all_gather(rotated[None], "grp", axis=0, tiled=True)
    result = result.astype(jnp.float32)
    return result.reshape(groups_count * AGG_DEV, block_width, slot_width * block_width)


def solution(mesh):
    return jax.shard_map(
        local,
        mesh=mesh,
        in_specs=(
            P(("grp", "dom"), None, None),
            P(("grp", "dom"), None, None),
            P(("grp", "dom"), None),
            P(("grp", "dom"), None),
            P(("grp", "dom")),
        ),
        out_specs=P("dom", None, None),
        check_vma=False,
    )
```

profile of v0, /device:TPU:1, one launch (start us, length us, event | category | flops | bytes accessed | tf_op | source)
XLA Modules:
  0.0 297.3 jit_solution(7769409100965928986)
XLA Ops:
  6.5 5.0 %collective-permute-start = (bf16[64,64,64]{2,1,0:T(8,128)(2,1)}, bf16[64,64,64]{2,1,0:T(8,128)(2,1)S(1)}, u32[]{:S(2)}, u32[]{:S(2)}) collective-permute-start(bf16[64,64,64]{2,1,0:T(8,128)(2,1)} %param.6), channel_id=1, source_target_pairs={{0,1},{1,2},{2,3},{3,4},{4,5},{5,6},{6,7},{7,8},{8,9},{9,10},{10,1... | collective-permute-start | bytes 1572872 | tf_op jit(solution)/shard_map/ppermute | solution.py:14
  11.6 1.9 collective-permute-start.1
  13.5 0.7 compare_and_fusion
  14.2 0.7 fusion.17
  15.0 0.7 fusion.22
  15.7 0.1 copy.14
  15.8 0.1 reshape.85
  15.9 0.1 copy.13
  16.0 19.7 %reshape.77 = bf16[64,64,12,64]{3,2,1,0:T(8,128)(2,1)} reshape(bf16[64,64,768]{2,1,0:T(8,128)(2,1)} %param.5) | data formatting | bytes 12582912 | tf_op jit(solution)/shard_map/reshape | solution.py:31
  35.7 0.1 copy.17
  36.5 0.1 copy.12
  36.6 4.2 %broadcast_multiply_fusion = bf16[64,64,4,64]{3,2,1,0:T(4,128)(2,1)} fusion(bf16[64,64,64]{2,1,0:T(8,128)(2,1)S(1)} %copy-done.1, bf16[64,4]{1,0:T(8,128)(2,1)S(1)} %copy.12), kind=kLoop, calls=%fused_computation.9 | loop fusion | flops 1048576 | bytes 2621952 | tf_op jit(solution)/shard_map/mul | solution.py:49
  40.8 7.0 %mul.38 = bf16[4096,256]{1,0:T(8,128)(2,1)} reshape(bf16[64,64,4,64]{3,2,1,0:T(4,128)(2,1)} %broadcast_multiply_fusion) | data formatting | bytes 4194304 | tf_op jit(solution)/shard_map/mul | solution.py:49
  47.8 0.0 collective-permute-done
  47.8 0.0 copy-start.2
  47.8 1.0 copy-done.2
  48.7 0.0 collective-permute-done.1
  48.7 2.2 pad_maximum_fusion
  51.0 18.2 %gather_fusion = bf16[768,64,64]{2,1,0:T(8,128)(2,1)} fusion(bf16[192,64,64]{2,1,0:T(8,128)(2,1)S(1)} %pad_maximum_fusion, s32[1024]{0:T(1024)S(1)} %pad_clamp_fusion), kind=kCustom, calls=%fused_computation | custom fusion | bytes 12585984 | tf_op jit(solution)/shard_map/jit(_take)/gather | solution.py:30
  69.1 16.6 %copy.15 = bf16[64,12,64,64]{2,3,1,0:T(8,128)(2,1)} copy(bf16[64,12,64,64]{3,2,1,0:T(8,128)(2,1)} %bitcast.19) | data formatting | bytes 12582912 | tf_op jit(solution)/shard_map/jit(_take)/gather | solution.py:30
  85.8 21.7 %fusion.4 = f32[64,64,12,64]{1,3,2,0:T(8,128)} fusion(bf16[64,64,12,64]{3,2,1,0:T(8,128)(2,1)} %reshape.77, bf16[64,12,64,64]{2,3,1,0:T(8,128)(2,1)} %copy.15, pred[64,12]{1,0:T(8,128)(4,1)S(1)} %copy.13), kind=kOutput, calls=%fused_computation.6 | convolution fusion | flops 405798912 | bytes 25166592 | tf_op jit(solution)/shard_map/ixky,ikyz->ixkz/dot_general | solution.py:32
  107.5 31.1 %copy.18 = f32[64,64,12,64]{3,2,1,0:T(8,128)} copy(f32[64,64,12,64]{1,3,2,0:T(8,128)} %fusion.4) | data formatting | bytes 25165824 | tf_op jit(solution)/shard_map/ixky,ikyz->ixkz/transpose | solution.py:32
  138.6 25.0 %convert_bitcast_fusion = bf16[64,64,12,64]{3,2,1,0:T(8,128)(2,1)} fusion(f32[64,64,12,64]{3,2,1,0:T(8,128)} %copy.18, s32[64,12]{1,0:T(8,128)S(1)} %copy.17, pred[64]{0:T(512)(128)(4,1)S(1)} %iota_compare_fusion.2), kind=kOutput, calls=%fused_computation.1 | convolution fusion | flops 456148992 | bytes 18877504 | tf_op jit(solution)/shard_map/ikt,ixkz->ixtz/dot_general | solution.py:40
  163.5 20.9 %reshape.98 = bf16[4096,768]{1,0:T(8,128)(2,1)} reshape(bf16[64,64,12,64]{3,2,1,0:T(8,128)(2,1)} %convert_bitcast_fusion) | data formatting | bytes 12582912 | tf_op jit(solution)/shard_map/reshape | solution.py:43
  184.4 4.6 %convolution_convert_fusion = bf16[256,768]{1,0:T(8,128)(2,1)S(1)} fusion(bf16[4096,256]{1,0:T(8,128)(2,1)S(1)} %copy-done, bf16[4096,768]{1,0:T(8,128)(2,1)} %reshape.98), kind=kOutput, calls=%fused_computation.10 | convolution fusion | flops 1610809344 | bytes 8781824 | tf_op jit(solution)/shard_map/dot_general | solution.py:51
  189.0 0.7 collective-permute-start.2
  189.7 0.0 collective-permute-done.2
  189.7 0.0 copy-start.3
  189.8 0.7 copy-done.3
  190.5 0.0 all-gather.3.cloned.1.call-update
  190.5 94.6 %all-gather.3.cloned.1.call-done = bf16[2048,768]{1,0:T(8,128)(2,1)} async-done(((bf16[256,768]{1,0:T(8,128)(2,1)}), bf16[2048,768]{1,0:T(8,128)(2,1)}) %all-gather.3.cloned.1.call-update) | async-done | bytes 3145744 | tf_op jit(solution)/shard_map/all_gather | solution.py:63
  285.1 5.4 %convert.1 = f32[32,64,768]{2,1,0:T(8,128)} convert(bf16[32,64,768]{2,1,0:T(8,128)(2,1)} %bitcast.20) | non-fusion elementwise | flops 1572864 | bytes 9437184 | tf_op jit(solution)/shard_map/reshape | solution.py:65
  (8 shorter events, 0.0 us)
Async XLA Ops:
  6.5 30.1 %copy-start.1 = (bf16[64,64,64]{2,1,0:T(8,128)(2,1)S(1)}, bf16[64,64,64]{2,1,0:T(8,128)(2,1)}, u32[]{:S(2)}) copy-start(bf16[64,64,64]{2,1,0:T(8,128)(2,1)} %param.6) | copy-start | bytes 1572868
  6.5 278.6 %all-gather.3.cloned.1.call-start = ((), (), s32[]{:S(2)}) async-start(), calls=%async_computation | async-start | bytes 3538944 | tf_op jit(solution)/shard_map/all_gather | solution.py:63
  6.5 41.2 %collective-permute-start = (bf16[64,64,64]{2,1,0:T(8,128)(2,1)}, bf16[64,64,64]{2,1,0:T(8,128)(2,1)S(1)}, u32[]{:S(2)}, u32[]{:S(2)}) collective-permute-start(bf16[64,64,64]{2,1,0:T(8,128)(2,1)} %param.6), channel_id=1, source_target_pairs={{0,1},{1,2},{2,3},{3,4},{4,5},{5,6},{6,7},{7,8},{8,9},{9,10},{10,1... | collective-permute-start | bytes 1572872 | tf_op jit(solution)/shard_map/ppermute | solution.py:14
  11.6 37.2 %collective-permute-start.1 = (bf16[64,64,64]{2,1,0:T(8,128)(2,1)}, bf16[64,64,64]{2,1,0:T(8,128)(2,1)}, u32[]{:S(2)}, u32[]{:S(2)}) collective-permute-start(bf16[64,64,64]{2,1,0:T(8,128)(2,1)} %param.6), channel_id=1, source_target_pairs={{1,0},{2,1},{3,2},{4,3},{5,4},{6,5},{7,6},{8,7},{9,8},{10,9},{11,1... | collective-permute-start | bytes 1572872 | tf_op jit(solution)/shard_map/ppermute | solution.py:17
  47.8 1.0 copy-start.2
  163.5 20.9 %copy-start = (bf16[4096,256]{1,0:T(8,128)(2,1)S(1)}, bf16[4096,256]{1,0:T(8,128)(2,1)}, u32[]{:S(2)}) copy-start(bf16[4096,256]{1,0:T(8,128)(2,1)} %mul.38) | copy-start | bytes 6291460
  189.0 0.7 collective-permute-start.2
  189.7 0.7 copy-start.3
Sparse Core Ops, SparseCore 0:
  190.6 94.4 all-gather.2
where the time goes:
time: 300 us; the launch traced here: 297 us
  local copies, waits for them, and re-layouts  116 us (39%)
  waiting for transfers between devices  94.6 us (32%)
  matrix products  51.3 us (17%)
  between operations  14.1 us (5%)
  other arithmetic  14 us (5%)
  starting transfers between devices  7.66 us (3%)
    all_gather x1, waiting for transfers between devices, local(): result = lax.all_gather(rotated[None], 'grp', axis=0, tiled=True)  94.6 us
    gather x2, local copies, waits for them, and re-layouts, local(): gathered = jnp.take(ghosts, local_rows, axis=0)  34.8 us
    transpose x1, local copies, waits for them, and re-layouts, local(): jnp.einsum('ixky,ikyz->ixkz', matrix_view, gathered, preferred_element_ty...  31.1 us
    dot_general x1, matrix products, local(): jnp.einsum('ikt,ixkz->ixtz', slot_select.astype(jnp.float32), products, p...  25 us
    dot_general x1, matrix products, local(): jnp.einsum('ixky,ikyz->ixkz', matrix_view, gathered, preferred_element_ty...  21.7 us
    reshape x1, local copies, waits for them, and re-layouts, local(): row_sums.astype(jnp.bfloat16)  20.9 us
    reshape x1, local copies, waits for them, and re-layouts, local(): fine_matrix_blocks.reshape(capacity, block_width, row_blocks, block_width)  19.7 us
    mul x1, local copies, waits for them, and re-layouts, local(): row_select.astype(jnp.bfloat16)[:, None, :, None]  6.95 us
  transfers between devices with their start and end apart: 4, of which 1 were waited for; matrix products, arithmetic and copies ran while one was open for 11% of the time, Pallas kernels for 0%

commit v1 on v0

--- a/solution.py
+++ b/solution.py
@@ -60,7 +60,11 @@
         for q in range(places)
     ]
     rotated = lax.ppermute(coarse.astype(jnp.bfloat16), ("grp", "dom"), pairs)
-    result = lax.all_gather(rotated[None], "grp", axis=0, tiled=True)
+    array_here = rotated[None]
+    p_next = lax.axis_size("grp")
+    mid_arr = jnp.stack(p_next * [array_here], 0)
+    r1 = lax.all_to_all(mid_arr, "grp", split_axis=0, concat_axis=0)
+    result = jnp.concatenate(r1, 0)
     result = result.astype(jnp.float32)
     return result.reshape(groups_count * AGG_DEV, block_width, slot_width * block_width)
 

time: 300 us -> 260 us (0.87)
  the two profiles are of different devices: /device:TPU:1 before, /device:TPU:96 now
where the time goes in v1:
time: 260 us; the launch traced here: 257 us
  local copies, waits for them, and re-layouts  115 us (44%)
  blocking collectives  71.4 us (27%)
  matrix products  51.3 us (20%)
  other arithmetic  12.1 us (5%)
  starting transfers between devices  6.37 us (2%)
    all_to_all x1, blocking collectives, local(): r1 = lax.all_to_all(mid_arr, 'grp', split_axis=0, concat_axis=0)  71.4 us
    gather x2, local copies, waits for them, and re-layouts, local(): gathered = jnp.take(ghosts, local_rows, axis=0)  34.8 us
    transpose x1, local copies, waits for them, and re-layouts, local(): jnp.einsum('ixky,ikyz->ixkz', matrix_view, gathered, preferred_element_ty...  31.1 us
    dot_general x1, matrix products, local(): jnp.einsum('ikt,ixkz->ixtz', slot_select.astype(jnp.float32), products, p...  25 us
    dot_general x1, matrix products, local(): jnp.einsum('ixky,ikyz->ixkz', matrix_view, gathered, preferred_element_ty...  21.7 us
    reshape x1, local copies, waits for them, and re-layouts, local(): row_sums.astype(jnp.bfloat16)  20.9 us
    reshape x1, local copies, waits for them, and re-layouts, local(): fine_matrix_blocks.reshape(capacity, block_width, row_blocks, block_width)  19.7 us
    mul x1, local copies, waits for them, and re-layouts, local(): row_select.astype(jnp.bfloat16)[:, None, :, None]  6.96 us
  transfers between devices with their start and end apart: 3, of which 0 were waited for; matrix products, arithmetic and copies ran while one was open for 13% of the time, Pallas kernels for 0%

profile of v1, /device:TPU:96, one launch (start us, length us, event | category | flops | bytes accessed | tf_op | source)
XLA Modules:
  0.0 257.1 jit_solution(11768309340637068309)
XLA Ops:
  0.0 2.0 collective-permute-start
  2.1 3.6 %collective-permute-start.1 = (bf16[64,64,64]{2,1,0:T(8,128)(2,1)}, bf16[64,64,64]{2,1,0:T(8,128)(2,1)}, u32[]{:S(2)}, u32[]{:S(2)}) collective-permute-start(bf16[64,64,64]{2,1,0:T(8,128)(2,1)} %param.6), channel_id=1, source_target_pairs={{1,0},{2,1},{3,2},{4,3},{5,4},{6,5},{7,6},{8,7},{9,8},{10,9},{11,1... | collective-permute-start | bytes 1572872 | tf_op jit(solution)/shard_map/ppermute | solution.py:17
  5.7 0.7 compare_and_fusion
  6.4 0.7 fusion.17
  7.1 0.7 fusion.22
  7.8 0.1 copy.21
  7.9 0.1 reshape.83
  8.0 0.1 copy.20
  8.2 19.7 %reshape.78 = bf16[64,64,12,64]{3,2,1,0:T(8,128)(2,1)} reshape(bf16[64,64,768]{2,1,0:T(8,128)(2,1)} %param.5) | data formatting | bytes 12582912 | tf_op jit(solution)/shard_map/reshape | solution.py:31
  27.9 0.1 copy.24
  28.7 0.1 copy.19
  28.8 0.0 copy-done.1
  28.8 4.2 %broadcast_multiply_fusion = bf16[64,64,4,64]{3,2,1,0:T(4,128)(2,1)} fusion(bf16[64,64,64]{2,1,0:T(8,128)(2,1)S(1)} %copy-done.1, bf16[64,4]{1,0:T(8,128)(2,1)S(1)} %copy.19), kind=kLoop, calls=%fused_computation.9 | loop fusion | flops 1048576 | bytes 2621952 | tf_op jit(solution)/shard_map/mul | solution.py:49
  33.0 7.0 %mul.38 = bf16[4096,256]{1,0:T(8,128)(2,1)} reshape(bf16[64,64,4,64]{3,2,1,0:T(4,128)(2,1)} %broadcast_multiply_fusion) | data formatting | bytes 4194304 | tf_op jit(solution)/shard_map/mul | solution.py:49
  40.0 0.0 collective-permute-done
  40.0 0.0 copy-start.2
  40.0 1.0 copy-done.2
  41.0 0.0 collective-permute-done.1
  41.0 2.2 pad_maximum_fusion
  43.2 18.2 %gather_fusion = bf16[768,64,64]{2,1,0:T(8,128)(2,1)} fusion(bf16[192,64,64]{2,1,0:T(8,128)(2,1)S(1)} %pad_maximum_fusion, s32[1024]{0:T(1024)S(1)} %pad_clamp_fusion), kind=kCustom, calls=%fused_computation | custom fusion | bytes 12585984 | tf_op jit(solution)/shard_map/jit(_take)/gather | solution.py:30
  61.4 16.6 %copy.22 = bf16[64,12,64,64]{2,3,1,0:T(8,128)(2,1)} copy(bf16[64,12,64,64]{3,2,1,0:T(8,128)(2,1)} %bitcast.19) | data formatting | bytes 12582912 | tf_op jit(solution)/shard_map/jit(_take)/gather | solution.py:30
  78.0 21.7 %fusion.4 = f32[64,64,12,64]{1,3,2,0:T(8,128)} fusion(bf16[64,64,12,64]{3,2,1,0:T(8,128)(2,1)} %reshape.78, bf16[64,12,64,64]{2,3,1,0:T(8,128)(2,1)} %copy.22, pred[64,12]{1,0:T(8,128)(4,1)S(1)} %copy.20), kind=kOutput, calls=%fused_computation.6 | convolution fusion | flops 405798912 | bytes 25166592 | tf_op jit(solution)/shard_map/ixky,ikyz->ixkz/dot_general | solution.py:32
  99.7 31.1 %copy.25 = f32[64,64,12,64]{3,2,1,0:T(8,128)} copy(f32[64,64,12,64]{1,3,2,0:T(8,128)} %fusion.4) | data formatting | bytes 25165824 | tf_op jit(solution)/shard_map/ixky,ikyz->ixkz/transpose | solution.py:32
  130.8 25.0 %convert_bitcast_fusion = bf16[64,64,12,64]{3,2,1,0:T(8,128)(2,1)} fusion(f32[64,64,12,64]{3,2,1,0:T(8,128)} %copy.25, s32[64,12]{1,0:T(8,128)S(1)} %copy.24, pred[64]{0:T(512)(128)(4,1)S(1)} %iota_compare_fusion.2), kind=kOutput, calls=%fused_computation.1 | convolution fusion | flops 456148992 | bytes 18877504 | tf_op jit(solution)/shard_map/ikt,ixkz->ixtz/dot_general | solution.py:40
  155.8 20.9 %reshape.92 = bf16[4096,768]{1,0:T(8,128)(2,1)} reshape(bf16[64,64,12,64]{3,2,1,0:T(8,128)(2,1)} %convert_bitcast_fusion) | data formatting | bytes 12582912 | tf_op jit(solution)/shard_map/reshape | solution.py:43
  176.7 0.0 copy-done
  176.7 4.6 %convolution_convert_fusion = bf16[256,768]{1,0:T(8,128)(2,1)S(1)} fusion(bf16[4096,256]{1,0:T(8,128)(2,1)S(1)} %copy-done, bf16[4096,768]{1,0:T(8,128)(2,1)} %reshape.92), kind=kOutput, calls=%fused_computation.10 | convolution fusion | flops 1610809344 | bytes 8781824 | tf_op jit(solution)/shard_map/dot_general | solution.py:51
  181.3 0.7 collective-permute-start.2
  182.0 0.0 collective-permute-done.2
  182.0 0.2 stack.3
  182.2 71.4 %all_to_all.5 = bf16[8,1,256,768]{3,2,1,0:T(8,128)(2,1)S(1)} all-to-all(bf16[8,1,256,768]{3,2,1,0:T(8,128)(2,1)S(1)} %stack.3), channel_id=1, replica_groups=mesh['grp'=8,'dom'=32] {'grp'}, dimensions={0} | all-to-all | bytes 6291456 | tf_op jit(solution)/shard_map/all_to_all | solution.py:66
  253.6 3.5 %convert.1 = f32[32,64,768]{2,1,0:T(8,128)} convert(bf16[32,64,768]{2,1,0:T(8,128)(2,1)S(1)} %bitcast.20) | non-fusion elementwise | flops 1572864 | bytes 9437184 | tf_op jit(solution)/shard_map/convert_element_type | solution.py:68
  (5 shorter events, 0.0 us)
Async XLA Ops:
  0.0 28.8 %copy-start.1 = (bf16[64,64,64]{2,1,0:T(8,128)(2,1)S(1)}, bf16[64,64,64]{2,1,0:T(8,128)(2,1)}, u32[]{:S(2)}) copy-start(bf16[64,64,64]{2,1,0:T(8,128)(2,1)} %param.6) | copy-start | bytes 1572868
  0.0 40.0 %collective-permute-start = (bf16[64,64,64]{2,1,0:T(8,128)(2,1)}, bf16[64,64,64]{2,1,0:T(8,128)(2,1)S(1)}, u32[]{:S(2)}, u32[]{:S(2)}) collective-permute-start(bf16[64,64,64]{2,1,0:T(8,128)(2,1)} %param.6), channel_id=1, source_target_pairs={{0,1},{1,2},{2,3},{3,4},{4,5},{5,6},{6,7},{7,8},{8,9},{9,10},{10,1... | collective-permute-start | bytes 1572872 | tf_op jit(solution)/shard_map/ppermute | solution.py:14
  2.1 38.9 %collective-permute-start.1 = (bf16[64,64,64]{2,1,0:T(8,128)(2,1)}, bf16[64,64,64]{2,1,0:T(8,128)(2,1)}, u32[]{:S(2)}, u32[]{:S(2)}) collective-permute-start(bf16[64,64,64]{2,1,0:T(8,128)(2,1)} %param.6), channel_id=1, source_target_pairs={{1,0},{2,1},{3,2},{4,3},{5,4},{6,5},{7,6},{8,7},{9,8},{10,9},{11,1... | collective-permute-start | bytes 1572872 | tf_op jit(solution)/shard_map/ppermute | solution.py:17
  40.0 1.0 copy-start.2
  155.8 20.9 %copy-start = (bf16[4096,256]{1,0:T(8,128)(2,1)S(1)}, bf16[4096,256]{1,0:T(8,128)(2,1)}, u32[]{:S(2)}) copy-start(bf16[4096,256]{1,0:T(8,128)(2,1)} %mul.38) | copy-start | bytes 6291460
  181.3 0.7 collective-permute-start.2
